TPU v7x, 256 devices: a whole 4x4x8 slice. The times are simulated.
256 devices in a mesh: lat: 16 (over z_hi, y, core), lon: 16 (over x, z_lo).
Axes of the slice: x: 4, y: 4, z: 8 (z_hi: 2, z_lo: 4; z = z_hi * 4 + z_lo), core: 2. Of those that a mesh axis runs over, the one named last changes fastest.
Arguments:
- forward_state: float32 [256, 32768], P(None, ('lat', 'lon')), may hold values from -6 to 6
- adjoint_state: float32 [256, 32768], P(None, ('lat', 'lon')), may hold values from -6 to 6
- inc_forward: float32 [4, 256, 32768], P(None, None, ('lat', 'lon')), may hold values from -6 to 6
- inc_adjoint: float32 [4, 256, 32768], P(None, None, ('lat', 'lon')), may hold values from -6 to 6
- bulk_modulus: float32 [32768], P(('lat', 'lon')), may hold values from 0.5 to 2
- inverse_size: float32 [32768], P(('lat', 'lon')), may hold values from 0.7 to 1.4
- face_codes: int32 [4, 32768], P(None, ('lat', 'lon')), may hold values from 0 to 7
- block_map: int32 [32768], P(('lat', 'lon')), may hold values from 0 to 255
- probe_dirs: float32 [4, 256], P(None, ('lat', 'lon')), may hold values from -6 to 6
Outputs:
- new_forward: float32 [4, 256, 32768], P(None, None, ('lat', 'lon'))
- new_adjoint: float32 [4, 256, 32768], P(None, None, ('lat', 'lon'))
- hess_vec: float32 [4, 256], P(None, ('lat', 'lon'))
All inputs are finite; a program needn't handle non-finite values.
Results may differ from a plain program's by a relative error of at most 0.00013.
Values sent between devices are 32-bit elements; how exact they have to be, the bound alone decides.
No kernel may reach another device: no remote copies, remote signals or barrier semaphores. Data moves between devices by JAX's collectives and lax.ppermute only.
A program may use at most 64 MiB of HBM per device.

v0:
```python
import jax
import jax.numpy as jnp
import numpy as np
from jax import lax
from jax.sharding import PartitionSpec as P

TIME_STEP = 0.05
PENALTY = 1.0
LIFT_FACTOR = 6.0


def shifted(block, axis, distance):
    devices = range(lax.axis_size(axis))
    route = [(i - distance, i) for i in devices if i - distance in devices]
    return lax.ppermute(block, axis, route)


def from_behind(value, axis, steps):
    count = lax.axis_size(axis)
    pairs = [(source, (source + steps) % count) for source in range(count)]
    return lax.ppermute(value, axis, pairs)


def node_tables():
    spread = 1.0 / np.sqrt(5.0)
    points = np.array([-1.0, -spread, spread, 1.0])
    weights = np.array([1.0, 5.0, 5.0, 1.0]) / 6.0
    products = np.array(
        [np.prod([points[j] - points[k] for k in range(4) if k != j]) for j in range(4)]
    )
    derivative = np.zeros((4, 4))
    for i in range(4):
        for j in range(4):
            if i != j:
                derivative[i, j] = products[i] / products[j] / (points[i] - points[j])
        derivative[i, i] = np.sum([1.0 / (points[i] - points[k]) for k in range(4) if k != i])
    identity = np.eye(4)
    directional = [
        np.kron(derivative, np.kron(identity, identity)),
        np.kron(identity, np.kron(derivative, identity)),
        np.kron(identity, np.kron(identity, derivative)),
    ]
    coupling = np.zeros((256, 256))
    for d in range(3):
        coupling[64 * (d + 1) : 64 * (d + 2), 0:64] = directional[d].T
        coupling[0:64, 64 * (d + 1) : 64 * (d + 2)] = directional[d].T
    selects = np.zeros((256, 192))
    for f in range(6):
        d = f // 2
        for u in range(4):
            for v in range(4):
                position = [u, v]
                position.insert(d, 3 * (f % 2))
                node_id = 16 * position[0] + 4 * position[1] + position[2]
                selects[node_id, 32 * f + 4 * u + v] = 1.0
                selects[64 * (d + 1) + node_id, 32 * f + 16 + 4 * u + v] = 1.0
    orient = np.zeros((8, 32), np.int32)
    for q in range(8):
        for u in range(4):
            for v in range(4):
                source_u, source_v = (v, u) if q & 1 else (u, v)
                if q & 2:
                    source_u = 3 - source_u
                if q & 4:
                    source_v = 3 - source_v
                orient[q, 4 * u + v] = 4 * source_u + source_v
                orient[q, 16 + 4 * u + v] = 16 + 4 * source_u + source_v
    quadrature = np.kron(weights, np.kron(weights, weights))
    return (
        jnp.asarray(coupling, dtype=jnp.float32),
        jnp.asarray(selects, dtype=jnp.float32),
        orient,
        jnp.asarray(quadrature, dtype=jnp.float32),
    )


def volume_rate(states, coupling, bulk_modulus, inverse_size):
    mixed = jnp.einsum("cd,scr->sdr", coupling, states, precision=lax.Precision.HIGHEST)
    channel = lax.broadcasted_iota(jnp.int32, (256, 1), 0)
    factor = jnp.where(
        channel < 64, -(bulk_modulus * inverse_size)[None, :], -inverse_size[None, :]
    )
    return mixed * factor[None]


def face_term(own_trace, neighbour, bulk_modulus, inverse_size, normal_sign):
    jump_pressure = neighbour[:, :16] - own_trace[:, :16]
    jump_velocity = neighbour[:, 16:] - own_trace[:, 16:]
    modulus = bulk_modulus[None, None, :]
    lift_scale = LIFT_FACTOR * inverse_size[None, None, :]
    on_pressure = lift_scale * (
        -modulus * normal_sign * 0.5 * jump_velocity + 0.5 * PENALTY * jump_pressure
    )
    on_velocity = lift_scale * (-normal_sign * 0.5 * jump_pressure + 0.5 * PENALTY * jump_velocity)
    return jnp.concatenate([on_pressure, on_velocity], 1)


def radial_neighbours(rad_minus, rad_plus):
    below_trace = jnp.concatenate([jnp.zeros_like(rad_plus[..., :1]), rad_plus[..., :-1]], -1)
    above_trace = jnp.concatenate([rad_minus[..., 1:], jnp.zeros_like(rad_minus[..., :1])], -1)
    return (below_trace, above_trace)


def heun_step(states, sources, neighbour_fn, bulk_modulus, inverse_size, coupling, selects):

    def rate_of(field_now):
        traces_all = jnp.einsum("ck,scr->skr", selects, field_now, precision=lax.Precision.HIGHEST)
        traces = [traces_all[:, 32 * f : 32 * f + 32] for f in range(6)]
        neighbours = neighbour_fn(traces)
        face_rates = jnp.concatenate(
            [
                face_term(traces[f], neighbours[f], bulk_modulus, inverse_size, 2.0 * (f % 2) - 1.0)
                for f in range(6)
            ],
            1,
        )
        lifted = jnp.einsum("ck,skr->scr", selects, face_rates, precision=lax.Precision.HIGHEST)
        return volume_rate(field_now, coupling, bulk_modulus, inverse_size) + lifted + sources

    first_rate = rate_of(states)
    second_rate = rate_of(states + TIME_STEP * first_rate)
    return states + 0.5 * TIME_STEP * (first_rate + second_rate)


def divergence(field_state, coupling, inverse_size):
    return -inverse_size * jnp.einsum(
        "cn,...cr->...nr", coupling[:, :64], field_state, precision=lax.Precision.HIGHEST
    )


def pressure_source(perturb, forward_div, adjoint_div):
    source_terms = jnp.concatenate(
        [perturb[:, None, :] * forward_div[None], perturb[:, None, :] * adjoint_div[None]], 0
    )
    return jnp.concatenate(
        [source_terms, jnp.zeros((source_terms.shape[0], 192, source_terms.shape[2]), jnp.float32)],
        1,
    )


def sensitivity(
    new_forward, new_adjoint, forward_div, adjoint_state, inverse_size, coupling, quadrature
):
    new_div = divergence(new_forward, coupling, inverse_size)
    integrand = new_adjoint[:, :64] * forward_div[None] + adjoint_state[None, :64] * new_div
    return jnp.einsum("n,pnr->pr", quadrature, integrand, precision=lax.Precision.HIGHEST) / (
        64.0 * inverse_size**3
    )


def reorient(neighbour, codes_face, orient):
    result = jnp.zeros_like(neighbour)
    for code in range(8):
        permuted = neighbour[:, orient[code], :]
        result = result + jnp.where((codes_face == code)[None, None, :], permuted, 0.0)
    return result


def shift_lat(rim, offset):
    return shifted(rim, "lat", offset)


def shift_lon(rim, offset):
    return from_behind(rim, "lon", offset)


def rims_lat(first_rim, last_rim):
    from_south = shift_lat(last_rim, 1)
    from_north = shift_lat(first_rim, -1)
    return (from_south, from_north)


def rims_lon(first_rim, last_rim):
    from_west = shift_lon(last_rim, 1)
    from_east = shift_lon(first_rim, -1)
    return (from_west, from_east)


def body(
    forward_state,
    adjoint_state,
    inc_forward,
    inc_adjoint,
    bulk_modulus,
    inverse_size,
    face_codes,
    block_map,
    probe_dirs,
):
    coupling, selects, orient, quadrature = node_tables()
    whole_dirs = lax.all_gather(probe_dirs, ("lat", "lon"), axis=1, tiled=True)
    perturb = jnp.take(whole_dirs, block_map, axis=1)
    forward_div = divergence(forward_state, coupling, inverse_size)
    adjoint_div = divergence(adjoint_state, coupling, inverse_size)

    def neighbour_fn(traces):
        from_south, from_north = rims_lat(traces[0], traces[1])
        from_west, from_east = rims_lon(traces[2], traces[3])
        sides = [from_south, from_north, from_west, from_east]
        horizontal = [reorient(sides[f], face_codes[f], orient) for f in range(4)]
        below_trace, above_trace = radial_neighbours(traces[4], traces[5])
        return horizontal + [below_trace, above_trace]

    probe_count = inc_forward.shape[0]
    states = jnp.concatenate([inc_forward, inc_adjoint], 0)
    sources = pressure_source(perturb, forward_div, adjoint_div)
    updated = heun_step(
        states, sources, neighbour_fn, bulk_modulus, inverse_size, coupling, selects
    )
    new_forward = updated[:probe_count]
    new_adjoint = updated[probe_count:]
    element_terms = sensitivity(
        new_forward, new_adjoint, forward_div, adjoint_state, inverse_size, coupling, quadrature
    )
    partial_sums = jax.ops.segment_sum(
        element_terms.T, block_map, num_segments=whole_dirs.shape[1]
    ).T
    hess_vec = lax.psum_scatter(partial_sums, ("lat", "lon"), scatter_dimension=1, tiled=True)
    return (new_forward, new_adjoint, hess_vec)


def solution(mesh):
    placed = (
        P(None, ("lat", "lon")),
        P(None, ("lat", "lon")),
        P(None, None, ("lat", "lon")),
        P(None, None, ("lat", "lon")),
        P(("lat", "lon")),
        P(("lat", "lon")),
        P(None, ("lat", "lon")),
        P(("lat", "lon")),
        P(None, ("lat", "lon")),
    )
    return jax.shard_map(
        body,
        mesh=mesh,
        in_specs=placed,
        out_specs=(
            P(None, None, ("lat", "lon")),
            P(None, None, ("lat", "lon")),
            P(None, ("lat", "lon")),
        ),
        check_vma=False,
    )
```

profile of v0, /device:TPU:1, one launch (start us, length us, event | category | flops | bytes accessed | tf_op | source)
XLA Modules:
  0.0 863.0 jit_solution(8838339508929728169)
XLA Ops:
  4.5 7.4 collective-permute-start.3
  11.9 3.0 collective-permute-start.1
  14.9 3.1 collective-permute-start
  21.9 597.1 %all-gather = f32[256,1,4]{2,1,0:T(1,128)S(1)} all-gather(f32[1,1,4]{2,1,0:T(1,128)S(1)} %bitcast.171), channel_id=1, replica_groups=mesh['lat'=16,'lon'=16] {'lat','lon'}, dimensions={0}, use_global_device_ids=true | all-gather | bytes 4112 | tf_op jit(solution)/shard_map/all_gather | solution.py:191
  622.4 2.1 fusion.7
  627.0 1.2 gather_fusion.24
  628.3 1.2 gather_fusion.25
  631.7 1.2 gather_fusion.17
  633.0 1.3 gather_fusion.26
  634.2 1.2 gather_fusion.18
  635.5 1.2 gather_fusion.27
  636.7 1.2 gather_fusion.19
  637.9 1.2 gather_fusion.28
  639.2 1.3 gather_fusion.20
  642.9 1.3 gather_fusion.30
  644.1 1.2 gather_fusion.22
  646.6 1.2 gather_fusion.23
  649.4 1.2 gather_fusion.9
  650.7 1.2 gather_fusion.10
  651.9 1.3 gather_fusion.11
  653.2 1.2 gather_fusion.12
  654.4 1.3 gather_fusion.13
  655.6 1.2 gather_fusion.14
  656.9 1.2 gather_fusion.15
  659.1 1.2 gather_fusion
  660.3 1.2 gather_fusion.1
  661.6 1.2 gather_fusion.2
  664.1 1.2 gather_fusion.4
  666.5 1.2 gather_fusion.6
  667.8 1.2 gather_fusion.7
  669.7 1.5 bitcast_add_fusion.7
  680.6 2.2 fusion.8
  683.5 1.5 collective-permute-start.6
  684.9 33.6 %collective-permute-start.5 = (f32[8,32,128]{2,1,0:T(8,128)}, f32[8,32,128]{2,1,0:T(8,128)}, u32[]{:S(2)}, u32[]{:S(2)}) collective-permute-start(f32[8,32,128]{2,1,0:T(8,128)} %get-tuple-element.18), channel_id=1, source_target_pairs={{16,0},{32,16},{48,32},{64,48},{80,64},{96,80},{112,96},{128,112},... | collective-permute-start | bytes 393224 | tf_op jit(solution)/shard_map/ppermute | solution.py:15
  718.6 2.1 collective-permute-start.4
  723.9 1.2 gather_fusion.59
  725.2 1.2 gather_fusion.60
  726.4 1.2 gather_fusion.61
  727.6 1.3 gather_fusion.62
  728.9 1.2 gather_fusion.63
  732.4 1.2 gather_fusion.49
  733.6 1.3 gather_fusion.50
  734.8 1.2 gather_fusion.51
  736.1 1.2 gather_fusion.52
  738.6 1.3 gather_fusion.54
  739.8 1.2 gather_fusion.55
  741.0 1.3 gather_fusion.56
  743.3 1.2 gather_fusion.41
  744.5 1.2 gather_fusion.42
  745.8 1.2 gather_fusion.43
  747.0 1.2 gather_fusion.44
  749.5 1.2 gather_fusion.46
  750.7 1.2 gather_fusion.47
  752.0 1.2 gather_fusion.48
  754.2 1.2 gather_fusion.33
  755.4 1.2 gather_fusion.34
  757.9 1.2 gather_fusion.36
  760.4 1.2 gather_fusion.38
  761.6 1.2 gather_fusion.39
  762.8 1.2 gather_fusion.40
  764.2 1.6 bitcast_add_fusion.3
  772.1 1.3 fusion.4
  776.1 1.2 scatter_custom_fusion
  777.4 85.2 %all-reduce.5 = f32[4,256]{0,1:T(8,128)S(1)} all-reduce(f32[4,256]{0,1:T(8,128)S(1)} %bitcast.169), channel_id=2, replica_groups=mesh['lat'=16,'lon'=16] {'lat','lon'}, use_global_device_ids=true, to_apply=%region_1.2.clone | all-reduce | flops 1024 | bytes 8192
  (375 shorter events, 55.7 us)
Async XLA Ops:
  0.6 20.0 %copy-start = (f32[256,128]{1,0:T(8,128)S(1)}, f32[256,128]{1,0:T(8,128)}, u32[]{:S(2)}) copy-start(f32[256,128]{1,0:T(8,128)} %param.140) | copy-start | bytes 393220
  0.6 1.2 copy-start.61
  4.5 621.5 %collective-permute-start.3 = (f32[8,32,128]{2,1,0:T(8,128)}, f32[8,32,128]{2,1,0:T(8,128)}, u32[]{:S(2)}, u32[]{:S(2)}) collective-permute-start(f32[8,32,128]{2,1,0:T(8,128)} %get-tuple-element.22), channel_id=1, source_target_pairs={{0,15},{1,0},{2,1},{3,2},{4,3},{5,4},{6,5},{7,6},{8,7},{9,8},{10,9... | collective-permute-start | bytes 393224 | tf_op jit(solution)/shard_map/ppermute | solution.py:21
  11.9 6.1 copy-start.71
  11.9 617.6 %collective-permute-start.2 = (f32[8,32,128]{2,1,0:T(8,128)}, f32[8,32,128]{2,1,0:T(8,128)}, u32[]{:S(2)}, u32[]{:S(2)}) collective-permute-start(f32[8,32,128]{2,1,0:T(8,128)} %get-tuple-element.23), channel_id=1, source_target_pairs={{0,1},{1,2},{2,3},{3,4},{4,5},{5,6},{6,7},{7,8},{8,9},{9,10},{10,1... | collective-permute-start | bytes 393224 | tf_op jit(solution)/shard_map/ppermute | solution.py:21
  11.9 636.0 %collective-permute-start.1 = (f32[8,32,128]{2,1,0:T(8,128)}, f32[8,32,128]{2,1,0:T(8,128)}, u32[]{:S(2)}, u32[]{:S(2)}) collective-permute-start(f32[8,32,128]{2,1,0:T(8,128)} %get-tuple-element.24), channel_id=1, source_target_pairs={{16,0},{32,16},{48,32},{64,48},{80,64},{96,80},{112,96},{128,112},... | collective-permute-start | bytes 393224 | tf_op jit(solution)/shard_map/ppermute | solution.py:15
  14.9 643.3 %collective-permute-start = (f32[8,32,128]{2,1,0:T(8,128)}, f32[8,32,128]{2,1,0:T(8,128)}, u32[]{:S(2)}, u32[]{:S(2)}) collective-permute-start(f32[8,32,128]{2,1,0:T(8,128)} %get-tuple-element.25), channel_id=1, source_target_pairs={{0,16},{16,32},{32,48},{48,64},{64,80},{80,96},{96,112},{112,128},... | collective-permute-start | bytes 393224 | tf_op jit(solution)/shard_map/ppermute | solution.py:15
  19.3 1.3 copy-start.62
  20.6 601.7 %copy-start.68 = (f32[128]{0:T(128)}, f32[128]{0:T(128)S(1)}, u32[]{:S(2)}) copy-start(f32[128]{0:T(128)S(1)} %get-tuple-element.61) | copy-start | bytes 1540
  622.4 2.1 copy-start.3
  622.4 2.1 copy-start.70
  631.7 1.2 copy-start.67
  634.2 1.2 copy-start.66
  669.7 1.7 copy-start.59
  669.7 1.7 copy-start.60
  671.3 1.0 copy-start.54
  671.3 1.1 copy-start.55
  671.3 1.1 copy-start.109
  671.3 1.1 copy-start.111
  671.3 1.1 copy-start.113
  671.3 1.1 copy-start.115
  671.3 1.1 copy-start.117
  672.8 1.1 copy-start.39
  672.8 1.1 copy-start.93
  672.8 1.1 copy-start.95
  672.8 1.1 copy-start.97
  674.2 1.1 copy-start.23
  674.2 1.1 copy-start.77
  674.2 1.1 copy-start.79
  674.2 1.1 copy-start.81
  683.5 37.9 %collective-permute-start.7 = (f32[8,32,128]{2,1,0:T(8,128)S(1)}, f32[8,32,128]{2,1,0:T(8,128)S(1)}, u32[]{:S(2)}, u32[]{:S(2)}) collective-permute-start(f32[8,32,128]{2,1,0:T(8,128)S(1)} %get-tuple-element.16), channel_id=1, source_target_pairs={{0,15},{1,0},{2,1},{3,2},{4,3},{5,4},{6,5},{7,6},{8,7},{9,8},{10,9... | collective-permute-start | bytes 393224 | tf_op jit(solution)/shard_map/ppermute | solution.py:21
  683.5 47.9 %collective-permute-start.6 = (f32[8,32,128]{2,1,0:T(8,128)}, f32[8,32,128]{2,1,0:T(8,128)}, u32[]{:S(2)}, u32[]{:S(2)}) collective-permute-start(f32[8,32,128]{2,1,0:T(8,128)} %get-tuple-element.17), channel_id=1, source_target_pairs={{0,1},{1,2},{2,3},{3,4},{4,5},{5,6},{6,7},{7,8},{8,9},{9,10},{10,1... | collective-permute-start | bytes 393224 | tf_op jit(solution)/shard_map/ppermute | solution.py:21
  684.9 57.4 %collective-permute-start.5 = (f32[8,32,128]{2,1,0:T(8,128)}, f32[8,32,128]{2,1,0:T(8,128)}, u32[]{:S(2)}, u32[]{:S(2)}) collective-permute-start(f32[8,32,128]{2,1,0:T(8,128)} %get-tuple-element.18), channel_id=1, source_target_pairs={{16,0},{32,16},{48,32},{64,48},{80,64},{96,80},{112,96},{128,112},... | collective-permute-start | bytes 393224 | tf_op jit(solution)/shard_map/ppermute | solution.py:15
  718.6 34.6 %collective-permute-start.4 = (f32[8,32,128]{2,1,0:T(8,128)}, f32[8,32,128]{2,1,0:T(8,128)}, u32[]{:S(2)}, u32[]{:S(2)}) collective-permute-start(f32[8,32,128]{2,1,0:T(8,128)} %get-tuple-element.19), channel_id=1, source_target_pairs={{0,16},{16,32},{32,48},{48,64},{64,80},{80,96},{96,112},{112,128},... | collective-permute-start | bytes 393224 | tf_op jit(solution)/shard_map/ppermute | solution.py:15
  721.4 49.6 %copy-start.11 = (f32[8,32,127]{2,1,0:T(8,128)}, f32[8,32,127]{2,1,0:T(8,128)S(1)}, u32[]{:S(2)}) copy-start(f32[8,32,127]{2,1,0:T(8,128)S(1)} %get-tuple-element.14) | copy-start | bytes 390148
  762.8 1.3 copy-start.120
  762.8 1.3 copy-start.122
  762.8 1.3 copy-start.124
  762.8 1.3 copy-start.125
  764.1 1.8 copy-start.51
  764.1 1.8 copy-start.52
  764.1 1.8 copy-start.53
  764.1 1.8 copy-start.110
  764.1 1.8 copy-start.112
  764.1 1.8 copy-start.114
  764.2 1.8 copy-start.116
  764.2 1.8 copy-start.118
  765.8 1.1 copy-start.47
  765.9 1.1 copy-start.104
  765.9 1.1 copy-start.106
  765.9 1.1 copy-start.108
  767.3 1.1 copy-start.25
  767.3 1.1 copy-start.88
  767.3 1.1 copy-start.90
  767.3 1.1 copy-start.92
  768.7 1.1 copy-start.15
  768.7 1.1 copy-start.74
  768.8 1.1 copy-start.76
  768.8 1.1 copy-start.78
  770.0 1.9 copy-start.1
  771.0 1.1 copy-start.8
  773.4 1.1 slice-start
  773.4 1.1 copy-start.64
  773.4 1.1 copy-start.69
  (84 other events, 78.5 us)
where the time goes:
time: 864 us; the launch traced here: 863 us
  blocking collectives  682 us (79%)
  local copies, waits for them, and re-layouts  107 us (12%)
  starting transfers between devices  50.7 us (6%)
  other arithmetic  11.3 us (1%)
  matrix products  9.57 us (1%)
    all_gather x1, blocking collectives, body(): whole_dirs = lax.all_gather(probe_dirs, ('lat', 'lon'), axis=1, tiled=True)  597 us
    unnamed x1, blocking collectives  85.2 us
    gather x64, local copies, waits for them, and re-layouts, reorient(): permuted = neighbour[:, orient[code], :]  78.6 us
    ppermute x4, starting transfers between devices, shifted(): return lax.ppermute(block, axis, route)  41.9 us
  transfers between devices with their start and end apart: 8, of which 0 were waited for; matrix products, arithmetic and copies ran while one was open for 8% of the time, Pallas kernels for 0%

commit v1 on v0

--- a/solution.py
+++ b/solution.py
@@ -7,6 +7,18 @@
 TIME_STEP = 0.05
 PENALTY = 1.0
 LIFT_FACTOR = 6.0
+
+
+def tiles_measure(my_data):
+    return jnp.concatenate(
+        jax.lax.all_to_all(
+            jnp.stack(tuple((my_data for _ in range(jax.lax.axis_size(("lat", "lon")))))),
+            ("lat", "lon"),
+            0,
+            0,
+        ),
+        axis=1,
+    )
 
 
 def shifted(block, axis, distance):
@@ -188,7 +200,7 @@
     probe_dirs,
 ):
     coupling, selects, orient, quadrature = node_tables()
-    whole_dirs = lax.all_gather(probe_dirs, ("lat", "lon"), axis=1, tiled=True)
+    whole_dirs = tiles_measure(probe_dirs)
     perturb = jnp.take(whole_dirs, block_map, axis=1)
     forward_div = divergence(forward_state, coupling, inverse_size)
     adjoint_div = divergence(adjoint_state, coupling, inverse_size)

time: 864 us -> 257 us (0.30)
  blocking collectives: 682 us -> 83.4 us
  starting transfers between devices: 50.7 us -> 38.5 us
    all_gather x1 -> x0, blocking collectives: 597 us -> none  [body(): whole_dirs = lax.all_gather(probe_dirs, ('lat', 'lon'), axis=1, tiled=True)]
    ppermute x4, starting transfers between devices: 41.9 us -> 11.8 us  [shifted(): return lax.ppermute(block, axis, route)]
    all_to_all x0 -> x1, starting transfers between devices: none -> 16.7 us  [tiles_measure(): jax.lax.all_to_all(jnp.stack(tuple((my_data for _ in range(jax.lax.axis_s...]
  transfers between devices with their start and end apart: 8 -> 9, of which waited for: 0 -> 1; matrix products, arithmetic and copies ran while one was open for 8% -> 29% of each run, Pallas kernels for 0% -> 0%
where the time goes in v1:
time: 257 us; the launch traced here: 256 us
  local copies, waits for them, and re-layouts  106 us (41%)
  blocking collectives  83.4 us (32%)
  starting transfers between devices  38.5 us (15%)
  other arithmetic  13.7 us (5%)
  matrix products  8.59 us (3%)
  waiting for transfers between devices  3.37 us (1%)
    unnamed x1, blocking collectives  83.4 us
    gather x64, local copies, waits for them, and re-layouts, reorient(): permuted = neighbour[:, orient[code], :]  78.3 us
    all_to_all x1, starting transfers between devices, tiles_measure(): jax.lax.all_to_all(jnp.stack(tuple((my_data for _ in range(jax.lax.axis_s...  16.7 us
    unnamed x290, local copies, waits for them, and re-layouts  14.5 us
    ppermute x4, starting transfers between devices, shifted(): return lax.ppermute(block, axis, route)  11.8 us
    ppermute x4, starting transfers between devices, from_behind(): return lax.ppermute(value, axis, pairs)  10 us
  transfers between devices with their start and end apart: 9, of which 1 were waited for; matrix products, arithmetic and copies ran while one was open for 29% of the time, Pallas kernels for 0%

profile of v1, /device:TPU:1, one launch (start us, length us, event | category | flops | bytes accessed | tf_op | source)
XLA Modules:
  0.0 256.2 jit_solution(18142124840605071247)
XLA Ops:
  4.5 7.4 %collective-permute-start.3 = (f32[8,32,128]{2,1,0:T(8,128)}, f32[8,32,128]{2,1,0:T(8,128)}, u32[]{:S(2)}, u32[]{:S(2)}) collective-permute-start(f32[8,32,128]{2,1,0:T(8,128)} %get-tuple-element.22), channel_id=1, source_target_pairs={{0,15},{1,0},{2,1},{3,2},{4,3},{5,4},{6,5},{7,6},{8,7},{9,8},{10,9... | collective-permute-start | bytes 393224 | tf_op jit(solution)/shard_map/ppermute | solution.py:33
  11.9 2.9 %collective-permute-start.1 = (f32[8,32,128]{2,1,0:T(8,128)}, f32[8,32,128]{2,1,0:T(8,128)}, u32[]{:S(2)}, u32[]{:S(2)}) collective-permute-start(f32[8,32,128]{2,1,0:T(8,128)} %get-tuple-element.24), channel_id=1, source_target_pairs={{16,0},{32,16},{48,32},{64,48},{80,64},{96,80},{112,96},{128,112},... | collective-permute-start | bytes 393224 | tf_op jit(solution)/shard_map/ppermute | solution.py:27
  14.7 3.1 %collective-permute-start = (f32[8,32,128]{2,1,0:T(8,128)}, f32[8,32,128]{2,1,0:T(8,128)}, u32[]{:S(2)}, u32[]{:S(2)}) collective-permute-start(f32[8,32,128]{2,1,0:T(8,128)} %get-tuple-element.25), channel_id=1, source_target_pairs={{0,16},{16,32},{32,48},{48,64},{64,80},{80,96},{96,112},{112,128},... | collective-permute-start | bytes 393224 | tf_op jit(solution)/shard_map/ppermute | solution.py:27
  18.6 16.7 %all-to-all-start = ((f32[256,4,1]{1,2,0:T(1,128)}), f32[256,4,1]{1,2,0:T(1,128)}, u32[]{:S(2)}, u32[]{:S(2)}) async-start(f32[256,4,1]{1,2,0:T(1,128)} %stack.2), calls=%async_computation | async-start | bytes 262144 | tf_op jit(solution)/shard_map/all_to_all | solution.py:14
  44.1 3.3 %all-to-all-done = f32[256,4,1]{1,2,0:T(1,128)} async-done(((f32[256,4,1]{1,2,0:T(1,128)}), f32[256,4,1]{1,2,0:T(1,128)}, u32[]{:S(2)}, u32[]{:S(2)}) %all-to-all-start) | async-done | bytes 4128 | tf_op jit(solution)/shard_map/all_to_all | solution.py:14
  47.5 1.7 gather_fusion.32
  51.1 1.2 gather_fusion.24
  52.3 1.2 gather_fusion.25
  54.5 1.2 gather_fusion.16
  55.8 1.2 gather_fusion.17
  57.0 1.2 gather_fusion.26
  59.5 1.2 gather_fusion.27
  60.7 1.2 gather_fusion.19
  61.9 1.2 gather_fusion.28
  63.2 1.2 gather_fusion.20
  64.4 1.2 gather_fusion.29
  65.7 1.2 gather_fusion.21
  68.1 1.2 gather_fusion.22
  69.4 1.2 gather_fusion.31
  70.6 1.2 gather_fusion.23
  73.4 1.2 gather_fusion.9
  75.9 1.2 gather_fusion.11
  77.1 1.2 gather_fusion.12
  78.4 1.2 gather_fusion.13
  80.8 1.2 gather_fusion.15
  84.3 1.2 gather_fusion.1
  86.7 1.2 gather_fusion.3
  88.0 1.2 gather_fusion.4
  90.4 1.2 gather_fusion.6
  91.7 1.2 gather_fusion.7
  93.6 1.5 bitcast_add_fusion.7
  104.5 2.2 fusion.8
  107.3 2.6 %collective-permute-start.7 = (f32[8,32,128]{2,1,0:T(8,128)S(1)}, f32[8,32,128]{2,1,0:T(8,128)S(1)}, u32[]{:S(2)}, u32[]{:S(2)}) collective-permute-start(f32[8,32,128]{2,1,0:T(8,128)S(1)} %get-tuple-element.16), channel_id=1, source_target_pairs={{0,15},{1,0},{2,1},{3,2},{4,3},{5,4},{6,5},{7,6},{8,7},{9,8},{10,9... | collective-permute-start | bytes 393224 | tf_op jit(solution)/shard_map/ppermute | solution.py:33
  110.0 2.6 %collective-permute-start.5 = (f32[8,32,128]{2,1,0:T(8,128)}, f32[8,32,128]{2,1,0:T(8,128)}, u32[]{:S(2)}, u32[]{:S(2)}) collective-permute-start(f32[8,32,128]{2,1,0:T(8,128)} %get-tuple-element.18), channel_id=1, source_target_pairs={{16,0},{32,16},{48,32},{64,48},{80,64},{96,80},{112,96},{128,112},... | collective-permute-start | bytes 393224 | tf_op jit(solution)/shard_map/ppermute | solution.py:27
  112.6 3.3 %collective-permute-start.4 = (f32[8,32,128]{2,1,0:T(8,128)}, f32[8,32,128]{2,1,0:T(8,128)}, u32[]{:S(2)}, u32[]{:S(2)}) collective-permute-start(f32[8,32,128]{2,1,0:T(8,128)} %get-tuple-element.19), channel_id=1, source_target_pairs={{0,16},{16,32},{32,48},{48,64},{64,80},{80,96},{96,112},{112,128},... | collective-permute-start | bytes 393224 | tf_op jit(solution)/shard_map/ppermute | solution.py:27
  116.6 1.2 gather_fusion.57
  117.8 1.2 gather_fusion.58
  120.3 1.2 gather_fusion.60
  121.5 1.2 gather_fusion.61
  122.8 1.2 gather_fusion.62
  124.0 1.2 gather_fusion.63
  125.3 1.2 gather_fusion.64
  127.5 1.2 gather_fusion.49
  129.9 1.2 gather_fusion.51
  131.2 1.2 gather_fusion.52
  132.4 1.2 gather_fusion.53
  133.6 1.2 gather_fusion.54
  134.9 1.2 gather_fusion.55
  136.1 1.2 gather_fusion.56
  139.6 1.2 gather_fusion.42
  140.8 1.2 gather_fusion.43
  143.3 1.2 gather_fusion.45
  147.0 1.2 gather_fusion.48
  149.2 1.2 gather_fusion.33
  150.4 1.2 gather_fusion.34
  151.7 1.2 gather_fusion.35
  152.9 1.2 gather_fusion.36
  154.1 1.2 gather_fusion.37
  156.6 1.2 gather_fusion.39
  157.8 1.2 gather_fusion.40
  159.2 1.6 bitcast_add_fusion.3
  167.1 1.3 fusion.4
  171.1 1.2 scatter_custom_fusion
  172.3 83.4 %all-reduce.5 = f32[4,256]{0,1:T(8,128)S(1)} all-reduce(f32[4,256]{0,1:T(8,128)S(1)} %bitcast.171), channel_id=2, replica_groups=mesh['lat'=16,'lon'=16] {'lat','lon'}, use_global_device_ids=true, to_apply=%region_1.2.clone | all-reduce | flops 1024 | bytes 8192
  (387 shorter events, 58.6 us)
Async XLA Ops:
  0.6 37.9 %copy-start = (f32[256,128]{1,0:T(8,128)S(1)}, f32[256,128]{1,0:T(8,128)}, u32[]{:S(2)}) copy-start(f32[256,128]{1,0:T(8,128)} %param.140) | copy-start | bytes 393220
  0.6 1.2 copy-start.62
  4.5 45.6 %collective-permute-start.3 = (f32[8,32,128]{2,1,0:T(8,128)}, f32[8,32,128]{2,1,0:T(8,128)}, u32[]{:S(2)}, u32[]{:S(2)}) collective-permute-start(f32[8,32,128]{2,1,0:T(8,128)} %get-tuple-element.22), channel_id=1, source_target_pairs={{0,15},{1,0},{2,1},{3,2},{4,3},{5,4},{6,5},{7,6},{8,7},{9,8},{10,9... | collective-permute-start | bytes 393224 | tf_op jit(solution)/shard_map/ppermute | solution.py:33
  11.9 41.7 %collective-permute-start.2 = (f32[8,32,128]{2,1,0:T(8,128)}, f32[8,32,128]{2,1,0:T(8,128)}, u32[]{:S(2)}, u32[]{:S(2)}) collective-permute-start(f32[8,32,128]{2,1,0:T(8,128)} %get-tuple-element.23), channel_id=1, source_target_pairs={{0,1},{1,2},{2,3},{3,4},{4,5},{5,6},{6,7},{7,8},{8,9},{9,10},{10,1... | collective-permute-start | bytes 393224 | tf_op jit(solution)/shard_map/ppermute | solution.py:33
  11.9 60.0 %collective-permute-start.1 = (f32[8,32,128]{2,1,0:T(8,128)}, f32[8,32,128]{2,1,0:T(8,128)}, u32[]{:S(2)}, u32[]{:S(2)}) collective-permute-start(f32[8,32,128]{2,1,0:T(8,128)} %get-tuple-element.24), channel_id=1, source_target_pairs={{16,0},{32,16},{48,32},{64,48},{80,64},{96,80},{112,96},{128,112},... | collective-permute-start | bytes 393224 | tf_op jit(solution)/shard_map/ppermute | solution.py:27
  14.7 3.1 %copy-start.131 = (f32[4,1]{0,1:T(1,128)S(1)}, f32[4,1]{0,1:T(1,128)}, u32[]{:S(2)}) copy-start(f32[4,1]{0,1:T(1,128)} %param.148) | copy-start | bytes 52
  14.7 67.3 %collective-permute-start = (f32[8,32,128]{2,1,0:T(8,128)}, f32[8,32,128]{2,1,0:T(8,128)}, u32[]{:S(2)}, u32[]{:S(2)}) collective-permute-start(f32[8,32,128]{2,1,0:T(8,128)} %get-tuple-element.25), channel_id=1, source_target_pairs={{0,16},{16,32},{32,48},{48,64},{64,80},{80,96},{96,112},{112,128},... | collective-permute-start | bytes 393224 | tf_op jit(solution)/shard_map/ppermute | solution.py:27
  18.6 16.7 %copy-start.75 = (s32[4,128]{1,0:T(4,128)S(1)}, s32[4,128]{1,0:T(4,128)}, u32[]{:S(2)}) copy-start(s32[4,128]{1,0:T(4,128)} %param.146) | copy-start | bytes 6148
  18.6 28.9 %all-to-all-start = ((f32[256,4,1]{1,2,0:T(1,128)}), f32[256,4,1]{1,2,0:T(1,128)}, u32[]{:S(2)}, u32[]{:S(2)}) async-start(f32[256,4,1]{1,2,0:T(1,128)} %stack.2), calls=%async_computation | async-start | bytes 262144 | tf_op jit(solution)/shard_map/all_to_all | solution.py:14
  36.6 1.4 copy-start.141
  36.6 1.4 copy-start.142
  36.6 1.9 copy-start.63
  37.4 1.4 copy-start.64
  38.5 3.8 %copy-start.73 = (f32[128]{0:T(128)}, f32[128]{0:T(128)S(1)}, u32[]{:S(2)}) copy-start(f32[128]{0:T(128)S(1)} %get-tuple-element.61) | copy-start | bytes 1540
  38.5 3.9 %copy-start.13 = (f32[256,256,1]{1,0,2:T(8,128)S(1)}, f32[256,256,1]{1,0,2:T(8,128)}, u32[]{:S(2)}) copy-start(f32[256,256,1]{1,0,2:T(8,128)} %constant.176) | copy-start | bytes 786436
  42.4 1.1 copy-start.3
  47.5 1.7 copy-start.133
  55.8 1.2 copy-start.68
  58.2 1.2 copy-start.67
  60.7 1.2 copy-start.70
  63.2 1.2 copy-start.69
  65.7 1.2 copy-start.72
  68.1 1.2 copy-start.71
  93.6 1.7 copy-start.60
  93.6 1.7 copy-start.61
  95.2 1.1 copy-start.56
  95.2 1.1 copy-start.113
  95.2 1.1 copy-start.115
  95.2 1.1 copy-start.117
  95.2 1.1 copy-start.119
  95.2 1.1 copy-start.121
  96.7 1.1 copy-start.40
  96.7 1.1 copy-start.97
  98.1 1.1 copy-start.24
  98.1 1.1 copy-start.81
  107.3 9.2 %collective-permute-start.7 = (f32[8,32,128]{2,1,0:T(8,128)S(1)}, f32[8,32,128]{2,1,0:T(8,128)S(1)}, u32[]{:S(2)}, u32[]{:S(2)}) collective-permute-start(f32[8,32,128]{2,1,0:T(8,128)S(1)} %get-tuple-element.16), channel_id=1, source_target_pairs={{0,15},{1,0},{2,1},{3,2},{4,3},{5,4},{6,5},{7,6},{8,7},{9,8},{10,9... | collective-permute-start | bytes 393224 | tf_op jit(solution)/shard_map/ppermute | solution.py:33
  110.0 16.5 %collective-permute-start.6 = (f32[8,32,128]{2,1,0:T(8,128)}, f32[8,32,128]{2,1,0:T(8,128)}, u32[]{:S(2)}, u32[]{:S(2)}) collective-permute-start(f32[8,32,128]{2,1,0:T(8,128)} %get-tuple-element.17), channel_id=1, source_target_pairs={{0,1},{1,2},{2,3},{3,4},{4,5},{5,6},{6,7},{7,8},{8,9},{9,10},{10,1... | collective-permute-start | bytes 393224 | tf_op jit(solution)/shard_map/ppermute | solution.py:33
  110.0 27.4 %collective-permute-start.5 = (f32[8,32,128]{2,1,0:T(8,128)}, f32[8,32,128]{2,1,0:T(8,128)}, u32[]{:S(2)}, u32[]{:S(2)}) collective-permute-start(f32[8,32,128]{2,1,0:T(8,128)} %get-tuple-element.18), channel_id=1, source_target_pairs={{16,0},{32,16},{48,32},{64,48},{80,64},{96,80},{112,96},{128,112},... | collective-permute-start | bytes 393224 | tf_op jit(solution)/shard_map/ppermute | solution.py:27
  112.6 35.6 %collective-permute-start.4 = (f32[8,32,128]{2,1,0:T(8,128)}, f32[8,32,128]{2,1,0:T(8,128)}, u32[]{:S(2)}, u32[]{:S(2)}) collective-permute-start(f32[8,32,128]{2,1,0:T(8,128)} %get-tuple-element.19), channel_id=1, source_target_pairs={{0,16},{16,32},{32,48},{48,64},{64,80},{80,96},{96,112},{112,128},... | collective-permute-start | bytes 393224 | tf_op jit(solution)/shard_map/ppermute | solution.py:27
  116.5 49.4 %copy-start.11 = (f32[8,32,127]{2,1,0:T(8,128)}, f32[8,32,127]{2,1,0:T(8,128)S(1)}, u32[]{:S(2)}) copy-start(f32[8,32,127]{2,1,0:T(8,128)S(1)} %get-tuple-element.14) | copy-start | bytes 390148
  157.8 1.3 copy-start.124
  157.8 1.3 copy-start.126
  157.8 1.3 copy-start.128
  157.8 1.3 copy-start.129
  159.1 1.8 copy-start.52
  159.1 1.8 copy-start.53
  159.1 1.8 copy-start.54
  159.1 1.8 copy-start.114
  159.1 1.8 copy-start.116
  159.1 1.8 copy-start.118
  159.2 1.8 copy-start.120
  159.2 1.8 copy-start.122
  160.8 1.1 copy-start.48
  160.9 1.1 copy-start.108
  160.9 1.1 copy-start.110
  160.9 1.1 copy-start.112
  162.3 1.1 copy-start.26
  162.3 1.1 copy-start.92
  163.7 1.1 copy-start.16
  163.7 1.1 copy-start.78
  165.0 1.9 copy-start.1
  166.0 1.1 copy-start.8
  168.4 1.1 slice-start
  168.4 1.1 copy-start.65
  (90 other events, 85.6 us)
